TPU v7x, 256 devices: a whole 4x4x8 slice. The times are simulated.
256 devices in a mesh: grp: 16 (over y, x_lo, core), tm: 16 (over z, x_hi).
Axes of the slice: x: 4 (x_hi: 2, x_lo: 2; x = x_hi * 2 + x_lo), y: 4, z: 8, core: 2. Of those that a mesh axis runs over, the one named last changes fastest.
Arguments:
- motion: bfloat16 [1024, 128, 1024], P(('grp', 'tm')), may hold values from -30 to 30
- modulation: float32 [6, 1024], replicated, may hold values from -1.25 to 1.25
- w_temporal_qkv: bfloat16 [1024, 3072], replicated, may hold values from -1 to 1
- w_temporal_out: bfloat16 [1024, 1024], replicated, may hold values from -0.1875 to 0.1875
- w_inter_qkv: bfloat16 [1024, 3072], P('tm'), may hold values from -1 to 1
- w_inter_out: bfloat16 [1024, 1024], P('tm'), may hold values from -0.1875 to 0.1875
- links: int32 [16, 4], replicated, may hold values from 0 to 1, as said below
Outputs:
- motion_out: bfloat16 [1024, 128, 1024], P(('grp', 'tm'))
Inputs may be any that keep to these rules, and one draw needn't show every extreme that they name: Every group has between 1 and 4 links; one group has all of them and another exactly one.
All inputs are finite; a program needn't handle non-finite values.
Results may differ from a plain program's by a relative error of at most 0.008.
Values may be sent and summed in bfloat16 or wider, within the bound.
No kernel may reach another device: no remote copies, remote signals or barrier semaphores. Data moves between devices by JAX's collectives and lax.ppermute only.
A program may use at most 128 MiB of HBM per device.

v0:
```python
import jax
import jax.numpy as jnp
from jax import lax
from jax.sharding import PartitionSpec as P

HEAD = 64
REACH = 2
EPSILON = 1e-06


def from_behind(block, axis, distance):
    devices = range(lax.axis_size(axis))
    route = [((i - distance) % len(devices), i) for i in devices]
    return lax.ppermute(block, axis, route)


def modulate(field, modulation, first, second):
    values = field.astype(jnp.float32)
    mean_square = jnp.mean(values * values, axis=-1, keepdims=True)
    scaled = (
        values * lax.rsqrt(mean_square + EPSILON) * (1.0 + modulation[second]) + modulation[first]
    )
    return scaled.astype(jnp.bfloat16)


def softmax_rows(scores):
    row_top = jnp.max(scores, axis=-1, keepdims=True)
    weights = jnp.exp(scores - row_top)
    return (weights / jnp.sum(weights, axis=-1, keepdims=True)).astype(jnp.bfloat16)


def temporal_heads(char_items, qkv_weight):
    item_count, frame_count, feature_width = char_items.shape
    head_count = feature_width // HEAD
    packed = jnp.dot(
        char_items.reshape(item_count * frame_count, feature_width),
        qkv_weight,
        preferred_element_type=jnp.float32,
    )
    packed = packed.astype(jnp.bfloat16).reshape(item_count, frame_count, 3, head_count, HEAD)
    scores = jnp.einsum(
        "nfhd,nghd->nhfg", packed[:, :, 0], packed[:, :, 1], preferred_element_type=jnp.float32
    ) * HEAD ** (-0.5)
    weights = softmax_rows(scores)
    mixed_heads = jnp.einsum(
        "nhfg,nghd->nfhd", weights, packed[:, :, 2], preferred_element_type=jnp.float32
    )
    return mixed_heads.astype(jnp.bfloat16).reshape(item_count, frame_count, feature_width)


def per_device(motion, modulation, w_temporal_qkv, w_temporal_out, w_inter_qkv, w_inter_out, links):
    own_chars, all_frames, feature_width = motion.shape
    head_count = feature_width // HEAD
    inter_qkv, inter_out = (
        lax.all_gather(w_inter_qkv, "tm", axis=0, tiled=True),
        lax.all_gather(w_inter_out, "tm", axis=0, tiled=True),
    )
    normed = modulate(motion, modulation, 0, 1)
    t_mixed = temporal_heads(normed, w_temporal_qkv)
    t_projected = jnp.dot(
        t_mixed.reshape(own_chars * all_frames, feature_width),
        w_temporal_out,
        preferred_element_type=jnp.float32,
    )
    middle = (
        motion.astype(jnp.float32)
        + modulation[2] * t_projected.reshape(own_chars, all_frames, feature_width)
    ).astype(jnp.bfloat16)
    middle_frames = lax.all_to_all(middle, "tm", split_axis=1, concat_axis=0, tiled=True)
    char_count, frame_count, unused_width = middle_frames.shape
    token_count = char_count * frame_count
    normed_inter = modulate(middle_frames, modulation, 3, 4)
    packed = jnp.dot(
        normed_inter.reshape(token_count, feature_width),
        inter_qkv,
        preferred_element_type=jnp.float32,
    )
    packed = packed.astype(jnp.bfloat16).reshape(char_count, frame_count, 3 * feature_width)
    own_pairs = packed[:, :, feature_width:]
    neighbours = []
    current = own_pairs
    for step in range(REACH):
        current = from_behind(current, "grp", -1)
        neighbours.append(current)
    current = own_pairs
    for step in range(REACH):
        current = from_behind(current, "grp", 1)
        neighbours.append(current)
    stacked = jnp.concatenate([own_pairs] + neighbours, axis=0)
    queries = packed[:, :, :feature_width].reshape(char_count, frame_count, head_count, HEAD)
    key_part = stacked[:, :, :feature_width].reshape(-1, frame_count, head_count, HEAD)
    value_part = stacked[:, :, feature_width:].reshape(-1, frame_count, head_count, HEAD)
    scores = jnp.einsum(
        "cfhd,kfhd->fhck", queries, key_part, preferred_element_type=jnp.float32
    ) * HEAD ** (-0.5)
    group_ids = jnp.arange(links.shape[0], dtype=jnp.int32)
    own_links = jnp.sum(jnp.where(group_ids[:, None] == lax.axis_index("grp"), links, 0), axis=0)
    allowed = jnp.concatenate([jnp.ones((1,), jnp.int32), own_links])
    key_mask = jnp.repeat(allowed, char_count) > 0
    scores = jnp.where(key_mask, scores, -jnp.inf)
    weights = softmax_rows(scores)
    mixed_heads = jnp.einsum(
        "fhck,kfhd->cfhd", weights, value_part, preferred_element_type=jnp.float32
    ).astype(jnp.bfloat16)
    mixed_chars = lax.all_to_all(
        mixed_heads.reshape(char_count, frame_count, feature_width),
        "tm",
        split_axis=0,
        concat_axis=1,
        tiled=True,
    )
    result = jnp.dot(
        mixed_chars.reshape(own_chars * all_frames, feature_width),
        inter_out,
        preferred_element_type=jnp.float32,
    )
    total = middle.astype(jnp.float32) + modulation[5] * result.reshape(
        own_chars, all_frames, feature_width
    )
    return total.astype(jnp.bfloat16)


def solution(mesh):
    placed = (P(("grp", "tm"), None, None), P(), P(), P(), P("tm", None), P("tm", None), P())
    return jax.shard_map(
        per_device,
        mesh=mesh,
        in_specs=placed,
        out_specs=P(("grp", "tm"), None, None),
        check_vma=False,
    )
```

profile of v0, /device:TPU:16, one launch (start us, length us, event | category | flops | bytes accessed | tf_op | source)
XLA Modules:
  0.0 351.3 jit_solution(12227734614028227783)
XLA Ops:
  6.5 0.7 all-gather.3.cloned.1.call-update
  7.3 1.5 fusion.14
  8.8 1.0 fusion.53
  9.8 1.6 fusion.17
  11.4 7.6 %convolution_convert_fusion.1 = bf16[512,3072]{1,0:T(8,128)(2,1)} fusion(bf16[512,1024]{1,0:T(8,128)(2,1)S(1)} %bitcast.66, bf16[1024,3072]{1,0:T(8,128)(2,1)} %param.9), kind=kOutput, calls=%fused_computation.11 | convolution fusion | flops 3222798336 | bytes 10485760 | tf_op jit(solution)/shard_map/dot_general | solution.py:35
  19.0 8.6 %reshape.111 = bf16[4,128,3,16,64]{4,3,2,1,0:T(8,128)(2,1)} reshape(bf16[512,3072]{1,0:T(8,128)(2,1)} %convolution_convert_fusion.1) | data formatting | bytes 6291456 | tf_op jit(solution)/shard_map/reshape | solution.py:40
  27.6 6.1 %fusion.51 = (bf16[4,128,1,16,64]{4,3,2,1,0:T(8,128)(2,1)}, bf16[4,128,1,16,64]{4,3,2,1,0:T(8,128)(2,1)}, bf16[4,128,1,16,64]{4,3,2,1,0:T(8,128)(2,1)}) fusion(bf16[4,128,3,16,64]{4,3,2,1,0:T(8,128)(2,1)} %reshape.111), kind=kLoop, calls=%fused_computation.67 | loop fusion | bytes 6291456 | tf_op jit(solution)/shard_map/slice | solution.py:46
  33.7 2.8 copy.62
  36.5 3.5 %copy.63 = bf16[4,128,1,16,64]{1,4,3,0,2:T(8,128)(2,1)} copy(bf16[4,128,1,16,64]{4,3,2,1,0:T(8,128)(2,1)} %get-tuple-element.9) | data formatting | bytes 2097152
  40.1 3.6 %copy.61 = bf16[4,128,1,16,64]{1,4,3,0,2:T(8,128)(2,1)} copy(bf16[4,128,1,16,64]{4,3,2,1,0:T(8,128)(2,1)} %get-tuple-element.7) | data formatting | bytes 2097152
  43.6 2.0 fusion.42
  45.6 4.0 %fusion.54 = (f32[4,16,128]{2,1,0:T(8,128)S(1)}, f32[4,16,128,128]{2,3,1,0:T(8,128)S(1)}) fusion(f32[4,16,128,128]{2,3,1,0:T(8,128)S(1)} %fusion.42), kind=kOutput, calls=%fused_computation.70 | output fusion | flops 4194431 | bytes 8421376 | tf_op jit(solution)/shard_map/sub | solution.py:28
  49.7 0.7 fusion.40
  50.4 0.5 copy-done.2
  50.9 1.3 fusion.18
  52.2 0.8 copy.48
  53.0 48.2 %all_to_all.24 = bf16[4,128,1024]{2,0,1:T(4,128)(2,1)S(1)} all-to-all(bf16[4,128,1024]{2,0,1:T(4,128)(2,1)S(1)} %copy.48), channel_id=1, replica_groups=mesh['grp'=16,'tm'=16] {'tm'}, dimensions={1} | all-to-all | bytes 2097152 | tf_op jit(solution)/shard_map/all_to_all | solution.py:69
  101.2 0.4 convert_bitcast_fusion
  101.6 1.5 copy.50
  103.1 0.4 fusion.13
  103.5 0.1 reshape.107
  103.6 0.1 rsqrt.21
  103.7 1.9 fusion.23
  105.6 33.3 %all-gather.3.cloned.1.call-done = bf16[1024,3072]{1,0:T(8,128)(2,1)} async-done(((bf16[64,3072]{1,0:T(8,128)(2,1)}), bf16[1024,3072]{1,0:T(8,128)(2,1)}) %all-gather.3.cloned.1.call-update) | async-done | bytes 6291472 | tf_op jit(solution)/shard_map/all_gather | solution.py:55
  138.9 6.4 %fusion.7 = bf16[64,8,3072]{2,1,0:T(8,128)(2,1)S(1)} fusion(bf16[512,1024]{1,0:T(8,128)(2,1)S(1)} %fusion.23, bf16[1024,3072]{1,0:T(8,128)(2,1)} %all-gather.3.cloned.1.call-done), kind=kOutput, calls=%fused_computation.14 | convolution fusion | flops 3222798336 | bytes 10485760 | tf_op jit(solution)/shard_map/dot_general | solution.py:73
  145.3 1.7 copy-done.3
  147.0 1.9 fusion.52
  148.9 0.5 collective-permute-start.2
  149.4 45.5 %collective-permute-done = bf16[64,8,2048]{2,1,0:T(8,128)(2,1)} collective-permute-done((bf16[64,8,2048]{2,1,0:T(8,128)(2,1)S(1)}, bf16[64,8,2048]{2,1,0:T(8,128)(2,1)}, u32[]{:S(2)}, u32[]{:S(2)}) %collective-permute-start) | collective-permute-done | bytes 2097184 | tf_op jit(solution)/shard_map/ppermute | solution.py:14
  194.9 2.9 collective-permute-start.1
  197.9 0.1 select_reduce_fusion
  198.2 0.1 gt.12
  198.3 1.3 slice.57
  199.5 2.5 reshape.99
  202.1 3.1 constant_dynamic-update-slice_fusion.3
  205.2 39.5 %collective-permute-done.1 = bf16[64,8,2048]{2,1,0:T(8,128)(2,1)} collective-permute-done((bf16[64,8,2048]{2,1,0:T(8,128)(2,1)}, bf16[64,8,2048]{2,1,0:T(8,128)(2,1)}, u32[]{:S(2)}, u32[]{:S(2)}) %collective-permute-start.1) | collective-permute-done | bytes 2097184 | tf_op jit(solution)/shard_map/ppermute | solution.py:14
  244.7 3.2 constant_dynamic-update-slice_fusion.2
  247.9 3.2 constant_dynamic-update-slice_fusion.1
  251.0 3.2 constant_dynamic-update-slice_fusion
  254.2 9.3 %fusion.50 = (bf16[320,8,1024]{2,1,0:T(8,128)(2,1)}, bf16[320,8,1024]{2,1,0:T(8,128)(2,1)}) fusion(bf16[320,8,2048]{2,1,0:T(8,128)(2,1)} %constant_dynamic-update-slice_fusion), kind=kLoop, calls=%fused_computation.66 | loop fusion | bytes 20971520 | tf_op jit(solution)/shard_map/slice | solution.py:91
  263.6 8.7 %copy.53 = bf16[320,8,1024]{0,2,1:T(8,128)(2,1)} copy(bf16[320,8,1024]{2,1,0:T(8,128)(2,1)} %get-tuple-element.5) | data formatting | bytes 10485760 | tf_op jit(solution)/shard_map/slice | solution.py:91
  272.2 12.4 %fusion.55 = (f32[8,16,64]{2,1,0:T(8,128)S(1)}, f32[8,16,64,320]{3,2,1,0:T(8,128)}) fusion(pred[320]{0:T(512)(128)(4,1)S(1)} %gt.12, bf16[320,8,16,64]{0,3,2,1:T(8,128)(2,1)} %bitcast.63, bf16[64,8,16,64]{3,2,1,0:T(8,128)(2,1)S(1)} %copy-done.4), kind=kOutput, calls=%fused_computation.71 | convolution fusion | flops 346030400 | bytes 16810304 | tf_op jit(solution)/shard_map/sub | solution.py:28
  284.6 8.5 %copy.52 = bf16[320,8,1024]{0,2,1:T(8,128)(2,1)} copy(bf16[320,8,1024]{2,1,0:T(8,128)(2,1)} %get-tuple-element.6) | data formatting | bytes 10485760 | tf_op jit(solution)/shard_map/slice | solution.py:92
  293.1 8.8 %fusion.28 = bf16[8,16,64,64]{3,2,1,0:T(8,128)(2,1)S(1)} fusion(bf16[320,8,16,64]{0,3,2,1:T(8,128)(2,1)} %bitcast.64, f32[8,16,64,320]{3,2,1,0:T(8,128)} %get-tuple-element.21, f32[8,16,64]{2,1,0:T(8,128)S(1)} %get-tuple-element.20), kind=kOutput, calls=%fused_computation.40 | convolution fusion | flops 341311488 | bytes 16809984 | tf_op jit(solution)/shard_map/fhck,kfhd->cfhd/dot_general | solution.py:102
  301.9 2.4 copy.55
  304.3 4.9 %all-to-all-start.1 = ((bf16[64,8,1024]{2,1,0:T(8,128)(2,1)}), bf16[64,8,1024]{2,1,0:T(8,128)(2,1)}, u32[]{:S(2)}, u32[]{:S(2)}) async-start(bf16[64,8,1024]{2,1,0:T(8,128)(2,1)} %copy.55), calls=%async_computation.1 | async-start | bytes 2097152 | tf_op jit(solution)/shard_map/all_to_all | solution.py:105
  309.3 31.0 %all-to-all-done.1 = bf16[64,8,1024]{2,1,0:T(8,128)(2,1)} async-done(((bf16[64,8,1024]{2,1,0:T(8,128)(2,1)}), bf16[64,8,1024]{2,1,0:T(8,128)(2,1)}, u32[]{:S(2)}, u32[]{:S(2)}) %all-to-all-start.1) | async-done | bytes 1048608 | tf_op jit(solution)/shard_map/all_to_all | solution.py:105
  340.3 4.1 %add_convert_fusion = bf16[4,128,1024]{2,1,0:T(8,128)(2,1)} fusion(bf16[4,128,1024]{2,1,0:T(8,128)(2,1)S(1)} %fusion.18, bf16[1024,1024]{1,0:T(8,128)(2,1)} %all-gather.5.cloned.1.call-done, bf16[4,16,8,1024]{3,2,0,1:T(8,128)(2,1)} %bitcast.23, f32[1024]{0:T(1024)S(1)} %bitcast.72), kind=kOutput, calls=%fused_computation.37 | convolution fusion | flops 1075838976 | bytes 5246976 | tf_op jit(solution)/shard_map/dot_general | solution.py:112
  (26 shorter events, 0.3 us)
Async XLA Ops:
  6.5 43.8 %copy-start = (bf16[1024,1024]{1,0:T(8,128)(2,1)S(1)}, bf16[1024,1024]{1,0:T(8,128)(2,1)}, u32[]{:S(2)}) copy-start(bf16[1024,1024]{1,0:T(8,128)(2,1)} %param.10) | copy-start | bytes 6291460
  6.5 132.4 %all-gather.3.cloned.1.call-start = ((), (), s32[]{:S(2)}) async-start(), calls=%async_computation.2 | async-start | bytes 6684672 | tf_op jit(solution)/shard_map/all_gather | solution.py:55
  7.3 302.0 %all-gather.5.cloned.1.call-start = ((), (), s32[]{:S(2)}) async-start(), calls=%async_computation.3 | async-start | bytes 2228224 | tf_op jit(solution)/shard_map/all_gather | solution.py:56
  45.6 4.0 %copy-start.5 = (bf16[4,128,1,16,64]{1,4,3,0,2:T(8,128)(2,1)S(1)}, bf16[4,128,1,16,64]{1,4,3,0,2:T(8,128)(2,1)}, u32[]{:S(2)}) copy-start(bf16[4,128,1,16,64]{1,4,3,0,2:T(8,128)(2,1)} %copy.61) | copy-start | bytes 3145732
  49.7 1.2 copy-start.2
  145.3 1.7 copy-start.3
  147.0 50.8 %copy-start.6 = (s32[16,4]{0,1:T(4,128)S(1)}, s32[16,4]{0,1:T(4,128)}, u32[]{:S(2)}) copy-start(s32[16,4]{0,1:T(4,128)} %param.13) | copy-start | bytes 772
  148.9 46.0 %collective-permute-start = (bf16[64,8,2048]{2,1,0:T(8,128)(2,1)S(1)}, bf16[64,8,2048]{2,1,0:T(8,128)(2,1)}, u32[]{:S(2)}, u32[]{:S(2)}) collective-permute-start(bf16[64,8,2048]{2,1,0:T(8,128)(2,1)S(1)} %get-tuple-element.10), channel_id=1, source_target_pairs={{16,0},{32,16},{48,32},{64,48},{80,64},{96,80},{112,96},{128,112},... | collective-permute-start | bytes 6291464 | tf_op jit(solution)/shard_map/ppermute | solution.py:14
  148.9 48.9 %collective-permute-start.2 = (bf16[64,8,2048]{2,1,0:T(8,128)(2,1)S(1)}, bf16[64,8,2048]{2,1,0:T(8,128)(2,1)}, u32[]{:S(2)}, u32[]{:S(2)}) collective-permute-start(bf16[64,8,2048]{2,1,0:T(8,128)(2,1)S(1)} %get-tuple-element.10), channel_id=1, source_target_pairs={{240,0},{0,16},{16,32},{32,48},{48,64},{64,80},{80,96},{96,112},{1... | collective-permute-start | bytes 6291464 | tf_op jit(solution)/shard_map/ppermute | solution.py:14
  194.9 49.8 %collective-permute-start.1 = (bf16[64,8,2048]{2,1,0:T(8,128)(2,1)}, bf16[64,8,2048]{2,1,0:T(8,128)(2,1)}, u32[]{:S(2)}, u32[]{:S(2)}) collective-permute-start(bf16[64,8,2048]{2,1,0:T(8,128)(2,1)} %collective-permute-done), channel_id=1, source_target_pairs={{16,0},{32,16},{48,32},{64,48},{80,64},{96,80},{112,96},{128,112},... | collective-permute-start | bytes 6291464 | tf_op jit(solution)/shard_map/ppermute | solution.py:14
  197.8 53.2 %collective-permute-start.3 = (bf16[64,8,2048]{2,1,0:T(8,128)(2,1)}, bf16[64,8,2048]{2,1,0:T(8,128)(2,1)}, u32[]{:S(2)}, u32[]{:S(2)}) collective-permute-start(bf16[64,8,2048]{2,1,0:T(8,128)(2,1)} %collective-permute-done.2), channel_id=1, source_target_pairs={{240,0},{0,16},{16,32},{32,48},{48,64},{64,80},{80,96},{96,112},{1... | collective-permute-start | bytes 6291464 | tf_op jit(solution)/shard_map/ppermute | solution.py:14
  263.6 8.7 %copy-start.4 = (bf16[64,8,16,64]{3,2,1,0:T(8,128)(2,1)S(1)}, bf16[64,8,16,64]{3,2,1,0:T(8,128)(2,1)}, u32[]{:S(2)}) copy-start(bf16[64,8,16,64]{3,2,1,0:T(8,128)(2,1)} %reshape.99) | copy-start | bytes 3145732
  304.3 36.0 %all-to-all-start.1 = ((bf16[64,8,1024]{2,1,0:T(8,128)(2,1)}), bf16[64,8,1024]{2,1,0:T(8,128)(2,1)}, u32[]{:S(2)}, u32[]{:S(2)}) async-start(bf16[64,8,1024]{2,1,0:T(8,128)(2,1)} %copy.55), calls=%async_computation.1 | async-start | bytes 2097152 | tf_op jit(solution)/shard_map/all_to_all | solution.py:105
  309.2 35.2 %copy-start.1 = (bf16[1024,1024]{1,0:T(8,128)(2,1)S(1)}, bf16[1024,1024]{1,0:T(8,128)(2,1)}, u32[]{:S(2)}) copy-start(bf16[1024,1024]{1,0:T(8,128)(2,1)} %param.10) | copy-start | bytes 6291460
Sparse Core Ops, SparseCore 0:
  9.9 128.9 all-gather.2
  198.0 83.9 all-gather.4
where the time goes:
time: 353 us; the launch traced here: 351 us
  waiting for transfers between devices  150 us (42%)
  local copies, waits for them, and re-layouts  76.8 us (22%)
  blocking collectives  48.2 us (14%)
  matrix products  43.2 us (12%)
  between operations  13.6 us (4%)
  other arithmetic  11 us (3%)
  starting transfers between devices  8.41 us (2%)
    ppermute x4, waiting for transfers between devices, from_behind(): return lax.ppermute(block, axis, route)  85 us
    all_to_all x1, blocking collectives, per_device(): lax.all_to_all(middle, 'tm', split_axis=1, concat_axis=0, tiled=True)  48.2 us
    all_gather x1, waiting for transfers between devices, per_device(): lax.all_gather(w_inter_qkv, 'tm', axis=0, tiled=True)  33.3 us
    all_to_all x1, waiting for transfers between devices, per_device(): lax.all_to_all(mixed_heads.reshape(char_count, frame_count, feature_width...  31 us
    unnamed x20, local copies, waits for them, and re-layouts  21.7 us
    slice x2, local copies, waits for them, and re-layouts, per_device(): stacked[:, :, :feature_width].reshape(-1, frame_count, head_count, HEAD)  18 us
    sub x1, matrix products, softmax_rows(): weights = jnp.exp(scores - row_top)  12.4 us
    dot_general x1, matrix products, per_device(): jnp.einsum('fhck,kfhd->cfhd', weights, value_part, preferred_element_type...  8.79 us
  transfers between devices with their start and end apart: 7, of which 4 were waited for; matrix products, arithmetic and copies ran while one was open for 33% of the time, Pallas kernels for 0%

commit v1 on v0

--- a/solution.py
+++ b/solution.py
@@ -52,7 +52,9 @@
     own_chars, all_frames, feature_width = motion.shape
     head_count = feature_width // HEAD
     inter_qkv, inter_out = (
-        lax.all_gather(w_inter_qkv, "tm", axis=0, tiled=True),
+        jnp.concatenate(
+            lax.all_to_all(jnp.stack([w_inter_qkv] * lax.axis_size("tm")), "tm", 0, 0), axis=0
+        ),
         lax.all_gather(w_inter_out, "tm", axis=0, tiled=True),
     )
     normed = modulate(motion, modulation, 0, 1)

time: 353 us -> 458 us (1.30)
  waiting for transfers between devices: 150 us -> 258 us
  blocking collectives: 48.2 us -> 40.9 us
  starting transfers between devices: 8.41 us -> 13.4 us
    all_to_all x0 -> x1, waiting for transfers between devices: none -> 143 us  [per_device(): lax.all_to_all(jnp.stack([w_inter_qkv] * lax.axis_size('tm')), 'tm', 0, 0)]
    all_gather x1 -> x0, waiting for transfers between devices: 33.3 us -> none  [per_device(): lax.all_gather(w_inter_qkv, 'tm', axis=0, tiled=True)]
    all_to_all x1, blocking collectives: 48.2 us -> 40.9 us  [per_device(): lax.all_to_all(middle, 'tm', split_axis=1, concat_axis=0, tiled=True)]
    all_to_all x0 -> x1, starting transfers between devices: none -> 4.64 us  [per_device(): lax.all_to_all(jnp.stack([w_inter_qkv] * lax.axis_size('tm')), 'tm', 0, 0)]
  transfers between devices with their start and end apart: 7 -> 7, of which waited for: 4 -> 4; matrix products, arithmetic and copies ran while one was open for 33% -> 15% of each run, Pallas kernels for 0% -> 0%
where the time goes in v1:
time: 458 us; the launch traced here: 457 us
  waiting for transfers between devices  258 us (56%)
  local copies, waits for them, and re-layouts  77.2 us (17%)
  matrix products  45.6 us (10%)
  blocking collectives  40.9 us (9%)
  between operations  13.6 us (3%)
  starting transfers between devices  13.4 us (3%)
  other arithmetic  8.38 us (2%)
    all_to_all x1, waiting for transfers between devices, per_device(): lax.all_to_all(jnp.stack([w_inter_qkv] * lax.axis_size('tm')), 'tm', 0, 0)  143 us
    ppermute x4, waiting for transfers between devices, from_behind(): return lax.ppermute(block, axis, route)  85.2 us
    all_to_all x1, blocking collectives, per_device(): lax.all_to_all(middle, 'tm', split_axis=1, concat_axis=0, tiled=True)  40.9 us
    all_to_all x1, waiting for transfers between devices, per_device(): lax.all_to_all(mixed_heads.reshape(char_count, frame_count, feature_width...  29.3 us
    unnamed x20, local copies, waits for them, and re-layouts  20.5 us
    slice x2, local copies, waits for them, and re-layouts, per_device(): stacked[:, :, :feature_width].reshape(-1, frame_count, head_count, HEAD)  18.1 us
    sub x1, matrix products, softmax_rows(): weights = jnp.exp(scores - row_top)  12.4 us
  transfers between devices with their start and end apart: 7, of which 4 were waited for; matrix products, arithmetic and copies ran while one was open for 15% of the time, Pallas kernels for 0%

profile of v1, /device:TPU:16, one launch (start us, length us, event | category | flops | bytes accessed | tf_op | source)
XLA Modules:
  0.0 456.6 jit_solution(15010892530229111933)
XLA Ops:
  6.5 1.0 fusion.55
  7.6 1.5 fusion.13
  9.1 1.6 fusion.16
  10.7 7.6 %convolution_convert_fusion.1 = bf16[512,3072]{1,0:T(8,128)(2,1)} fusion(bf16[512,1024]{1,0:T(8,128)(2,1)S(1)} %bitcast.73, bf16[1024,3072]{1,0:T(8,128)(2,1)} %param.9), kind=kOutput, calls=%fused_computation.11 | convolution fusion | flops 3222798336 | bytes 10485760 | tf_op jit(solution)/shard_map/dot_general | solution.py:35
  18.3 8.6 %reshape.116 = bf16[4,128,3,16,64]{4,3,2,1,0:T(8,128)(2,1)} reshape(bf16[512,3072]{1,0:T(8,128)(2,1)} %convolution_convert_fusion.1) | data formatting | bytes 6291456 | tf_op jit(solution)/shard_map/reshape | solution.py:40
  26.9 6.0 %fusion.53 = (bf16[4,128,1,16,64]{4,3,2,1,0:T(8,128)(2,1)}, bf16[4,128,1,16,64]{4,3,2,1,0:T(8,128)(2,1)}, bf16[4,128,1,16,64]{4,3,2,1,0:T(8,128)(2,1)}) fusion(bf16[4,128,3,16,64]{4,3,2,1,0:T(8,128)(2,1)} %reshape.116), kind=kLoop, calls=%fused_computation.67 | loop fusion | bytes 6291456 | tf_op jit(solution)/shard_map/slice | solution.py:46
  32.9 2.8 copy.59
  35.7 3.5 copy.60
  39.3 2.0 fusion.44
  41.3 2.9 fusion.56
  44.2 2.8 copy.58
  47.1 3.0 fusion.42
  50.1 1.3 fusion.17
  51.3 0.8 copy.46
  52.2 40.9 %all_to_all.29 = bf16[4,128,1024]{2,0,1:T(4,128)(2,1)S(1)} all-to-all(bf16[4,128,1024]{2,0,1:T(4,128)(2,1)S(1)} %copy.46), channel_id=1, replica_groups=mesh['grp'=16,'tm'=16] {'tm'}, dimensions={1} | all-to-all | bytes 2097152 | tf_op jit(solution)/shard_map/all_to_all | solution.py:71
  93.0 3.4 stack.2
  96.5 4.6 %all-to-all-start.1 = ((bf16[16,64,3072]{2,1,0:T(8,128)(2,1)}), bf16[16,64,3072]{2,1,0:T(8,128)(2,1)}, u32[]{:S(2)}, u32[]{:S(2)}) async-start(bf16[16,64,3072]{2,1,0:T(8,128)(2,1)} %stack.2), calls=%async_computation.1 | async-start | bytes 12582912 | tf_op jit(solution)/shard_map/all_to_all | solution.py:56
  101.1 0.2 all-gather.2.cloned.1.call-start
  101.4 0.6 fusion.22
  102.0 0.5 fusion.25
  102.5 0.1 copy.48
  102.6 143.0 %all-to-all-done.1 = bf16[16,64,3072]{2,1,0:T(8,128)(2,1)} async-done(((bf16[16,64,3072]{2,1,0:T(8,128)(2,1)}), bf16[16,64,3072]{2,1,0:T(8,128)(2,1)}, u32[]{:S(2)}, u32[]{:S(2)}) %all-to-all-start.1) | async-done | bytes 6291488 | tf_op jit(solution)/shard_map/all_to_all | solution.py:56
  245.6 6.4 %fusion.7 = bf16[64,8,3072]{2,1,0:T(8,128)(2,1)S(1)} fusion(bf16[512,1024]{1,0:T(8,128)(2,1)S(1)} %bitcast.74, bf16[1024,3072]{1,0:T(8,128)(2,1)} %bitcast.17), kind=kOutput, calls=%fused_computation.14 | convolution fusion | flops 3222798336 | bytes 10485760 | tf_op jit(solution)/shard_map/dot_general | solution.py:75
  252.0 1.7 copy-done.3
  253.7 1.9 fusion.54
  255.6 0.5 collective-permute-start.2
  256.1 45.4 %collective-permute-done = bf16[64,8,2048]{2,1,0:T(8,128)(2,1)} collective-permute-done((bf16[64,8,2048]{2,1,0:T(8,128)(2,1)S(1)}, bf16[64,8,2048]{2,1,0:T(8,128)(2,1)}, u32[]{:S(2)}, u32[]{:S(2)}) %collective-permute-start) | collective-permute-done | bytes 2097184 | tf_op jit(solution)/shard_map/ppermute | solution.py:14
  301.5 2.9 collective-permute-start.1
  304.5 0.1 select_reduce_fusion
  304.6 0.1 add_compare_fusion
  304.7 0.1 broadcast_in_dim.34
  304.8 0.1 gt.12
  304.8 1.3 slice.57
  306.1 2.3 reshape.110
  308.5 3.1 constant_dynamic-update-slice_fusion.3
  311.6 39.8 %collective-permute-done.1 = bf16[64,8,2048]{2,1,0:T(8,128)(2,1)} collective-permute-done((bf16[64,8,2048]{2,1,0:T(8,128)(2,1)}, bf16[64,8,2048]{2,1,0:T(8,128)(2,1)}, u32[]{:S(2)}, u32[]{:S(2)}) %collective-permute-start.1) | collective-permute-done | bytes 2097184 | tf_op jit(solution)/shard_map/ppermute | solution.py:14
  351.4 3.1 constant_dynamic-update-slice_fusion.2
  354.5 3.2 constant_dynamic-update-slice_fusion.1
  357.7 3.2 constant_dynamic-update-slice_fusion
  360.9 9.3 %fusion.52 = (bf16[320,8,1024]{2,1,0:T(8,128)(2,1)}, bf16[320,8,1024]{2,1,0:T(8,128)(2,1)}) fusion(bf16[320,8,2048]{2,1,0:T(8,128)(2,1)} %constant_dynamic-update-slice_fusion), kind=kLoop, calls=%fused_computation.66 | loop fusion | bytes 20971520 | tf_op jit(solution)/shard_map/slice | solution.py:93
  370.3 8.7 %copy.50 = bf16[320,8,1024]{0,2,1:T(8,128)(2,1)} copy(bf16[320,8,1024]{2,1,0:T(8,128)(2,1)} %get-tuple-element.5) | data formatting | bytes 10485760 | tf_op jit(solution)/shard_map/slice | solution.py:93
  379.0 12.4 %fusion.57 = (f32[8,16,64]{2,1,0:T(8,128)S(1)}, f32[8,16,64,320]{3,2,1,0:T(8,128)}) fusion(pred[320]{0:T(512)(128)(4,1)S(1)} %gt.12, bf16[320,8,16,64]{0,3,2,1:T(8,128)(2,1)} %bitcast.70, bf16[64,8,16,64]{3,2,1,0:T(8,128)(2,1)S(1)} %copy-done.4), kind=kOutput, calls=%fused_computation.71 | convolution fusion | flops 346030400 | bytes 16810304 | tf_op jit(solution)/shard_map/sub | solution.py:28
  391.4 8.5 %copy.49 = bf16[320,8,1024]{0,2,1:T(8,128)(2,1)} copy(bf16[320,8,1024]{2,1,0:T(8,128)(2,1)} %get-tuple-element.6) | data formatting | bytes 10485760 | tf_op jit(solution)/shard_map/slice | solution.py:94
  399.9 8.8 %fusion.30 = bf16[8,16,64,64]{3,2,1,0:T(8,128)(2,1)S(1)} fusion(bf16[320,8,16,64]{0,3,2,1:T(8,128)(2,1)} %bitcast.71, f32[8,16,64,320]{3,2,1,0:T(8,128)} %get-tuple-element.21, f32[8,16,64]{2,1,0:T(8,128)S(1)} %get-tuple-element.20), kind=kOutput, calls=%fused_computation.40 | convolution fusion | flops 341311488 | bytes 16809984 | tf_op jit(solution)/shard_map/fhck,kfhd->cfhd/dot_general | solution.py:104
  408.7 2.4 copy.52
  411.1 5.1 %all-to-all-start.2 = ((bf16[64,8,1024]{2,1,0:T(8,128)(2,1)}), bf16[64,8,1024]{2,1,0:T(8,128)(2,1)}, u32[]{:S(2)}, u32[]{:S(2)}) async-start(bf16[64,8,1024]{2,1,0:T(8,128)(2,1)} %copy.52), calls=%async_computation.2 | async-start | bytes 2097152 | tf_op jit(solution)/shard_map/all_to_all | solution.py:107
  416.2 29.3 %all-to-all-done.2 = bf16[64,8,1024]{2,1,0:T(8,128)(2,1)} async-done(((bf16[64,8,1024]{2,1,0:T(8,128)(2,1)}), bf16[64,8,1024]{2,1,0:T(8,128)(2,1)}, u32[]{:S(2)}, u32[]{:S(2)}) %all-to-all-start.2) | async-done | bytes 1048608 | tf_op jit(solution)/shard_map/all_to_all | solution.py:107
  445.6 4.1 add_convert_fusion
  (22 shorter events, 0.1 us)
Async XLA Ops:
  6.5 43.5 %copy-start = (bf16[1024,1024]{1,0:T(8,128)(2,1)S(1)}, bf16[1024,1024]{1,0:T(8,128)(2,1)}, u32[]{:S(2)}) copy-start(bf16[1024,1024]{1,0:T(8,128)(2,1)} %param.10) | copy-start | bytes 6291460
  47.0 3.0 copy-start.2
  50.0 43.0 %copy-start.5 = (bf16[64,3072]{1,0:T(8,128)(2,1)S(1)}, bf16[64,3072]{1,0:T(8,128)(2,1)}, u32[]{:S(2)}) copy-start(bf16[64,3072]{1,0:T(8,128)(2,1)} %param.11) | copy-start | bytes 1179652
  96.5 149.1 %all-to-all-start.1 = ((bf16[16,64,3072]{2,1,0:T(8,128)(2,1)}), bf16[16,64,3072]{2,1,0:T(8,128)(2,1)}, u32[]{:S(2)}, u32[]{:S(2)}) async-start(bf16[16,64,3072]{2,1,0:T(8,128)(2,1)} %stack.2), calls=%async_computation.1 | async-start | bytes 12582912 | tf_op jit(solution)/shard_map/all_to_all | solution.py:56
  101.1 315.1 %all-gather.2.cloned.1.call-start = ((), (), s32[]{:S(2)}) async-start(), calls=%async_computation.3 | async-start | bytes 2228224 | tf_op jit(solution)/shard_map/all_gather | solution.py:58
  252.0 1.8 copy-start.3
  253.7 50.8 %copy-start.6 = (s32[16,4]{0,1:T(4,128)S(1)}, s32[16,4]{0,1:T(4,128)}, u32[]{:S(2)}) copy-start(s32[16,4]{0,1:T(4,128)} %param.13) | copy-start | bytes 772
  255.6 45.9 %collective-permute-start = (bf16[64,8,2048]{2,1,0:T(8,128)(2,1)S(1)}, bf16[64,8,2048]{2,1,0:T(8,128)(2,1)}, u32[]{:S(2)}, u32[]{:S(2)}) collective-permute-start(bf16[64,8,2048]{2,1,0:T(8,128)(2,1)S(1)} %get-tuple-element.10), channel_id=1, source_target_pairs={{16,0},{32,16},{48,32},{64,48},{80,64},{96,80},{112,96},{128,112},... | collective-permute-start | bytes 6291464 | tf_op jit(solution)/shard_map/ppermute | solution.py:14
  255.6 48.8 %collective-permute-start.2 = (bf16[64,8,2048]{2,1,0:T(8,128)(2,1)S(1)}, bf16[64,8,2048]{2,1,0:T(8,128)(2,1)}, u32[]{:S(2)}, u32[]{:S(2)}) collective-permute-start(bf16[64,8,2048]{2,1,0:T(8,128)(2,1)S(1)} %get-tuple-element.10), channel_id=1, source_target_pairs={{240,0},{0,16},{16,32},{32,48},{48,64},{64,80},{80,96},{96,112},{1... | collective-permute-start | bytes 6291464 | tf_op jit(solution)/shard_map/ppermute | solution.py:14
  301.5 49.9 %collective-permute-start.1 = (bf16[64,8,2048]{2,1,0:T(8,128)(2,1)}, bf16[64,8,2048]{2,1,0:T(8,128)(2,1)}, u32[]{:S(2)}, u32[]{:S(2)}) collective-permute-start(bf16[64,8,2048]{2,1,0:T(8,128)(2,1)} %collective-permute-done), channel_id=1, source_target_pairs={{16,0},{32,16},{48,32},{64,48},{80,64},{96,80},{112,96},{128,112},... | collective-permute-start | bytes 6291464 | tf_op jit(solution)/shard_map/ppermute | solution.py:14
  304.4 53.3 %collective-permute-start.3 = (bf16[64,8,2048]{2,1,0:T(8,128)(2,1)}, bf16[64,8,2048]{2,1,0:T(8,128)(2,1)}, u32[]{:S(2)}, u32[]{:S(2)}) collective-permute-start(bf16[64,8,2048]{2,1,0:T(8,128)(2,1)} %collective-permute-done.2), channel_id=1, source_target_pairs={{240,0},{0,16},{16,32},{32,48},{48,64},{64,80},{80,96},{96,112},{1... | collective-permute-start | bytes 6291464 | tf_op jit(solution)/shard_map/ppermute | solution.py:14
  370.2 8.7 %copy-start.4 = (bf16[64,8,16,64]{3,2,1,0:T(8,128)(2,1)S(1)}, bf16[64,8,16,64]{3,2,1,0:T(8,128)(2,1)}, u32[]{:S(2)}) copy-start(bf16[64,8,16,64]{3,2,1,0:T(8,128)(2,1)} %reshape.110) | copy-start | bytes 3145732
  411.1 34.5 %all-to-all-start.2 = ((bf16[64,8,1024]{2,1,0:T(8,128)(2,1)}), bf16[64,8,1024]{2,1,0:T(8,128)(2,1)}, u32[]{:S(2)}, u32[]{:S(2)}) async-start(bf16[64,8,1024]{2,1,0:T(8,128)(2,1)} %copy.52), calls=%async_computation.2 | async-start | bytes 2097152 | tf_op jit(solution)/shard_map/all_to_all | solution.py:107
  416.2 33.5 %copy-start.1 = (bf16[1024,1024]{1,0:T(8,128)(2,1)S(1)}, bf16[1024,1024]{1,0:T(8,128)(2,1)}, u32[]{:S(2)}) copy-start(bf16[1024,1024]{1,0:T(8,128)(2,1)} %param.10) | copy-start | bytes 6291460
Sparse Core Ops, SparseCore 0:
  304.6 84.0 all-gather.1
